TPU v7x, 32 devices: a whole 2x2x4 slice. The times are simulated.
32 devices in a mesh: task: 2 (over y), row: 4 (over z), col: 4 (over x, core).
Axes of the slice: x: 2, y: 2, z: 4, core: 2. Of those that a mesh axis runs over, the one named last changes fastest.
Arguments:
- features: bfloat16 [164, 4096], P(None, ('task', 'row', 'col')), parts along dimension 1, may hold values from -6 to 6
- rung_index: int32 [4096], P(('task', 'row', 'col')), parts along dimension 0, may hold values from 0 to 3
- w_first: bfloat16 [164, 512], replicated, may hold values from -0.5 to 0.5
- b_first: float32 [512], replicated, may hold values from -4 to 4
- w_second: bfloat16 [512, 512], replicated, may hold values from -0.25 to 0.25
- b_second: float32 [512], replicated, may hold values from -4 to 4
- w_third: bfloat16 [512, 64], replicated, may hold values from -0.25 to 0.25
- targets: float32 [16, 4096], P(None, ('task', 'row', 'col')), parts along dimension 1, may hold values from -80 to 80
- fidelity_factor: float32 [8, 4], P('task'), parts along dimension 0, may hold values from -4 to 4
- inverse_scale: float32 [2], P('task'), parts along dimension 0, may hold values from 0.02 to 0.1
- noise_var: float32 [2], P('task'), parts along dimension 0, may hold values from 0.3 to 1
Outputs:
- solution: float32 [16, 4096], P(None, ('task', 'row', 'col')), parts along dimension 1
- residual: float32 [16, 4096], P(None, ('task', 'row', 'col')), parts along dimension 1
There are 2 independent parts, one for each index of `task`. A program takes and returns all parts, laid end to end along the dimension named above; an argument that names none is the same for every part. Nothing has to cross between parts.
All inputs are finite; a program needn't handle non-finite values.
Results may differ from a plain program's by a relative error of at most 0.012.
The roundings to bfloat16 on the way count: a program that leaves them out, or rounds other values in their place, can miss the bound.
Values may be sent and summed in bfloat16 or wider, within the bound.
No kernel may reach another device: no remote copies, remote signals or barrier semaphores. Data moves between devices by JAX's collectives and lax.ppermute only.
A program may use at most 64 MiB of HBM per device.

v0:
```python
import jax
import jax.numpy as jnp
from jax import lax
from jax.sharding import PartitionSpec as P

ITERS = 2


def fidelity_matrix(fidelity_factor):
    lower = jnp.tril(fidelity_factor)
    return jnp.dot(lower, lower.T, precision=lax.Precision.HIGHEST) + 0.5 * jnp.eye(
        fidelity_factor.shape[0], dtype=jnp.float32
    )


def left_product(weights, values):
    return lax.dot_general(
        weights, values, (((0,), (0,)), ((), ())), preferred_element_type=jnp.float32
    )


def outer_gram(left_side, right_side):
    return lax.dot_general(
        left_side, right_side, (((1,), (1,)), ((), ())), precision=lax.Precision.HIGHEST
    )


def solve_spd(matrix, right_side):
    return jax.scipy.linalg.cho_solve((jnp.linalg.cholesky(matrix), True), right_side)


def block_size(total_count, largest):
    chosen = min(total_count, largest)
    while total_count % chosen != 0:
        chosen = chosen - 1
    return chosen


def one_hot_rows(rung_value, count_rungs):
    levels = jnp.arange(count_rungs, dtype=jnp.float32)
    return (rung_value.astype(jnp.float32)[:, None] == levels[None, :]).astype(jnp.float32)


def kernel_rows(
    row_embedding,
    row_squares,
    row_onehot,
    col_embedding,
    col_rung,
    direction,
    fidelity,
    inverse_scale,
):
    count_rows = row_embedding.shape[1]
    count_cols = col_embedding.shape[1]
    row_block = block_size(count_rows, 512)
    col_block = block_size(count_cols, 2048)
    col_squares = jnp.sum(jnp.square(col_embedding.astype(jnp.float32)), axis=0)
    col_fidelity = jnp.dot(
        fidelity, one_hot_rows(col_rung, fidelity.shape[0]).T, precision=lax.Precision.HIGHEST
    )

    def one_row_block(block_number):
        first_row = block_number * row_block
        rows_embedding = lax.dynamic_slice_in_dim(row_embedding, first_row, row_block, 1)
        rows_squares = lax.dynamic_slice_in_dim(row_squares, first_row, row_block, 0)
        rows_onehot = lax.dynamic_slice_in_dim(row_onehot, first_row, row_block, 0)

        def one_col_block(running, column_number):
            first_col = column_number * col_block
            cols_embedding = lax.dynamic_slice_in_dim(col_embedding, first_col, col_block, 1)
            cols_squares = lax.dynamic_slice_in_dim(col_squares, first_col, col_block, 0)
            cols_fidelity = lax.dynamic_slice_in_dim(col_fidelity, first_col, col_block, 1)
            cols_direction = lax.dynamic_slice_in_dim(direction, first_col, col_block, 1)
            inner = left_product(rows_embedding, cols_embedding)
            distance = rows_squares[:, None] + cols_squares[None, :] - 2.0 * inner
            tile_fidelity = jnp.dot(rows_onehot, cols_fidelity, precision=lax.Precision.HIGHEST)
            kernel = jnp.exp(-inverse_scale[0] * distance) * tile_fidelity
            contribution = lax.dot_general(
                cols_direction, kernel, (((1,), (1,)), ((), ())), precision=lax.Precision.HIGHEST
            )
            return (running + contribution, None)

        start_value = jnp.zeros((direction.shape[0], row_block), jnp.float32)
        result, unused = lax.scan(
            one_col_block, start_value, jnp.arange(count_cols // col_block, dtype=jnp.int32)
        )
        return result

    stacked = lax.map(one_row_block, jnp.arange(count_rows // row_block, dtype=jnp.int32))
    return jnp.transpose(stacked, (1, 0, 2)).reshape(direction.shape[0], count_rows)


def on_device(
    features,
    rung_index,
    w_first,
    b_first,
    w_second,
    b_second,
    w_third,
    targets,
    fidelity_factor,
    inverse_scale,
    noise_var,
):
    fidelity = fidelity_matrix(fidelity_factor)
    hidden_one = jax.nn.silu(left_product(w_first, features) + b_first[:, None]).astype(
        jnp.bfloat16
    )
    hidden_two = jax.nn.silu(left_product(w_second, hidden_one) + b_second[:, None]).astype(
        jnp.bfloat16
    )
    embedding = left_product(w_third, hidden_two).astype(jnp.bfloat16)
    rung_value = rung_index.astype(jnp.float32).astype(jnp.bfloat16)
    row_embedding, row_rung = (
        lax.all_gather(embedding, "col", axis=1, tiled=True),
        lax.all_gather(rung_value, "col", axis=0, tiled=True),
    )
    col_embedding, col_rung = (
        lax.all_gather(embedding, "row", axis=1, tiled=True),
        lax.all_gather(rung_value, "row", axis=0, tiled=True),
    )
    row_squares = jnp.sum(jnp.square(row_embedding.astype(jnp.float32)), axis=0)
    row_onehot = one_hot_rows(row_rung, fidelity.shape[0])
    solution = jnp.zeros_like(targets)
    residual = targets
    direction = targets
    gram = lax.psum(outer_gram(residual, residual), ("row", "col"))
    for iteration in range(ITERS):
        partial_value = kernel_rows(
            row_embedding,
            row_squares,
            row_onehot,
            col_embedding,
            col_rung,
            lax.all_gather(direction, "row", axis=1, tiled=True),
            fidelity,
            inverse_scale,
        )
        image = (
            lax.psum_scatter(partial_value, "col", scatter_dimension=1, tiled=True)
            + noise_var[0] * direction
        )
        curvature = lax.psum(outer_gram(direction, image), ("row", "col"))
        step_matrix = solve_spd(curvature, gram)
        solution = solution + jnp.dot(step_matrix.T, direction, precision=lax.Precision.HIGHEST)
        residual = residual - jnp.dot(step_matrix.T, image, precision=lax.Precision.HIGHEST)
        if iteration + 1 < ITERS:
            new_gram = lax.psum(outer_gram(residual, residual), ("row", "col"))
        if iteration + 1 < ITERS:
            update_matrix = solve_spd(gram, new_gram)
            direction = residual + jnp.dot(
                update_matrix.T, direction, precision=lax.Precision.HIGHEST
            )
            gram = new_gram
    return (solution, residual)


def solution(mesh):
    placed = (
        P(None, ("task", "row", "col")),
        P(("task", "row", "col")),
        P(),
        P(),
        P(),
        P(),
        P(),
        P(None, ("task", "row", "col")),
        P("task", None),
        P("task"),
        P("task"),
    )
    return jax.shard_map(
        on_device,
        mesh=mesh,
        in_specs=placed,
        out_specs=(P(None, ("task", "row", "col")), P(None, ("task", "row", "col"))),
        check_vma=False,
    )
```

profile of v0, /device:TPU:0, one launch (start us, length us, event | category | flops | bytes accessed | tf_op | source)
XLA Modules:
  0.0 256.6 jit_solution(4763473048253713967)
XLA Ops:
  7.2 1.3 multiply_convert_fusion.1
  9.1 13.7 %all_gather.19 = bf16[64,512]{1,0:T(8,128)(2,1)S(1)} all-gather(bf16[64,128]{1,0:T(8,128)(2,1)S(1)} %fusion.4), channel_id=1, replica_groups=mesh['task'=2,'row'=4,'col'=4] {'row'}, dimensions={1}, use_global_device_ids=true | all-gather | bytes 81920 | tf_op jit(solution)/shard_map/all_gather | solution.py:121
  22.8 5.4 %all_gather.18 = bf16[64,512]{1,0:T(8,128)(2,1)S(1)} all-gather(bf16[64,128]{1,0:T(8,128)(2,1)S(1)} %fusion.4), channel_id=1, replica_groups=mesh['task'=2,'row'=4,'col'=4] {'col'}, dimensions={1}, use_global_device_ids=true | all-gather | bytes 81920 | tf_op jit(solution)/shard_map/all_gather | solution.py:117
  28.2 9.8 %all-gather.1 = bf16[4,1,128]{2,1,0:T(2,128)(2,1)S(1)} all-gather(bf16[1,1,128]{2,1,0:T(2,128)(2,1)S(1)} %convert_bitcast_fusion), channel_id=1, replica_groups=mesh['task'=2,'row'=4,'col'=4] {'row'}, dimensions={0}, use_global_device_ids=true | all-gather | bytes 1280 | tf_op jit(solution)/shard_map/all_gather | solution.py:122
  38.0 5.0 %all-gather = bf16[4,1,128]{2,1,0:T(2,128)(2,1)S(1)} all-gather(bf16[1,1,128]{2,1,0:T(2,128)(2,1)S(1)} %convert_bitcast_fusion), channel_id=1, replica_groups=mesh['task'=2,'row'=4,'col'=4] {'col'}, dimensions={0}, use_global_device_ids=true | all-gather | bytes 1280 | tf_op jit(solution)/shard_map/all_gather | solution.py:118
  44.5 13.1 %all_gather.22 = f32[16,512]{1,0:T(8,128)S(1)} all-gather(f32[16,128]{1,0:T(8,128)S(1)} %copy-done.1), channel_id=1, replica_groups=mesh['task'=2,'row'=4,'col'=4] {'row'}, dimensions={1}, use_global_device_ids=true | all-gather | bytes 40960 | tf_op jit(solution)/shard_map/all_gather | solution.py:137
  59.0 1.6 convolution_bitcast_fusion
  61.5 17.0 %reduce-scatter.3.cloned.1.call-done = f32[16,128]{1,0:T(8,128)} async-done(((f32[16,512]{1,0:T(8,128)}), f32[16,128]{1,0:T(8,128)}) %reduce-scatter.3.cloned.1.call-update) | async-done | bytes 8208 | tf_op jit(solution)/shard_map/reduce_scatter | solution.py:142
  78.5 0.8 convolution_bitcast_fusion.1
  79.3 59.7 %all-reduce = (f32[16,16]{0,1:T(8,128)S(1)}, f32[16,16]{0,1:T(8,128)S(1)}) all-reduce(f32[16,16]{0,1:T(8,128)S(1)} %fusion.37, f32[16,16]{0,1:T(8,128)S(1)} %convolution_bitcast_fusion.1), channel_id=1, replica_groups=mesh['task'=2,'row'=4,'col'=4] {'row','col'}, use_global_device_ids=true, to_apply=%region_6.8 | all-reduce | flops 512 | bytes 4096 | tf_op jit(solution)/shard_map/psum | solution.py:129
  139.2 1.5 cholesky.70
  142.0 1.2 custom-call.10
  143.2 1.5 cholesky.59
  146.0 1.2 custom-call.9
  148.5 30.0 %psum.30 = f32[16,16]{1,0:T(8,128)S(1)} all-reduce(f32[16,16]{1,0:T(8,128)S(1)} %fusion.39), channel_id=1, replica_groups=mesh['task'=2,'row'=4,'col'=4] {'row','col'}, use_global_device_ids=true, to_apply=%region_7.10 | all-reduce | flops 256 | bytes 2048 | tf_op jit(solution)/shard_map/psum | solution.py:150
  179.0 13.1 %all_gather.23 = f32[16,512]{1,0:T(8,128)S(1)} all-gather(f32[16,128]{1,0:T(8,128)S(1)} %convolution_add_fusion.3), channel_id=1, replica_groups=mesh['task'=2,'row'=4,'col'=4] {'row'}, dimensions={1}, use_global_device_ids=true | all-gather | bytes 40960 | tf_op jit(solution)/shard_map/all_gather | solution.py:137
  192.1 1.6 fusion.40
  193.9 16.7 %reduce-scatter.5.cloned.1.call-done = f32[16,128]{1,0:T(8,128)} async-done(((f32[16,512]{1,0:T(8,128)}), f32[16,128]{1,0:T(8,128)}) %reduce-scatter.5.cloned.1.call-update) | async-done | bytes 8208 | tf_op jit(solution)/shard_map/reduce_scatter | solution.py:142
  210.7 0.8 fusion.28
  211.5 32.2 %psum.31 = f32[16,16]{0,1:T(8,128)S(1)} all-reduce(f32[16,16]{0,1:T(8,128)S(1)} %fusion.28), channel_id=1, replica_groups=mesh['task'=2,'row'=4,'col'=4] {'row','col'}, use_global_device_ids=true, to_apply=%region_9.12 | all-reduce | flops 256 | bytes 2048 | tf_op jit(solution)/shard_map/psum | solution.py:145
  243.8 1.5 cholesky.81
  246.6 1.2 custom-call.11
  248.1 0.8 convolution_add_fusion.2
  249.0 0.8 convolution_subtract_fusion
  (55 shorter events, 9.4 us)
Async XLA Ops:
  7.2 1.4 copy-start
  7.2 1.4 copy-start.5
  7.2 1.4 copy-start.4
  7.2 71.3 %reduce-scatter.3.cloned.1.call-start = ((), (), s32[]{:S(2)}) async-start(), calls=%async_computation.2 | async-start | bytes 40960 | tf_op jit(solution)/shard_map/reduce_scatter | solution.py:142
  22.8 5.4 %copy-start.7 = (s32[128]{0:T(128)S(1)}, s32[128]{0:T(128)}, u32[]{:S(2)}) copy-start(s32[128]{0:T(128)} %param.15) | copy-start | bytes 1540
  43.1 0.7 copy-start.6
  43.8 0.7 copy-start.1
  60.6 150.1 %reduce-scatter.5.cloned.1.call-start = ((), (), s32[]{:S(2)}) async-start(), calls=%async_computation.3 | async-start | bytes 40960 | tf_op jit(solution)/shard_map/reduce_scatter | solution.py:142
  147.4 0.7 copy-start.2
  248.1 0.8 copy-start.3
Sparse Core Ops, SparseCore 0:
  60.7 17.7 reduce-scatter.2
  193.9 16.7 reduce-scatter.4
where the time goes:
time: 257 us
  blocking collectives  182 us (71%)
  waiting for transfers between devices  33.8 us (13%)
  between operations  15.5 us (6%)
  other arithmetic  12.1 us (5%)
  matrix products  11.6 us (5%)
    psum x1, blocking collectives, on_device(): gram = lax.psum(outer_gram(residual, residual), ('row', 'col'))  59.7 us
    reduce_scatter x2, waiting for transfers between devices, on_device(): lax.psum_scatter(partial_value, 'col', scatter_dimension=1, tiled=True)  33.8 us
    psum x1, blocking collectives, on_device(): curvature = lax.psum(outer_gram(direction, image), ('row', 'col'))  32.2 us
    psum x1, blocking collectives, on_device(): new_gram = lax.psum(outer_gram(residual, residual), ('row', 'col'))  30 us
    all_gather x2, blocking collectives, on_device(): lax.all_gather(direction, 'row', axis=1, tiled=True)  26.2 us
    all_gather x1, blocking collectives, on_device(): lax.all_gather(embedding, 'row', axis=1, tiled=True)  13.7 us
    all_gather x1, blocking collectives, on_device(): lax.all_gather(rung_value, 'row', axis=0, tiled=True)  9.84 us
    another operation x9, other arithmetic, solve_spd(): jnp.linalg.cholesky(matrix)  6.39 us
  transfers between devices with their start and end apart: 2, of which 2 were waited for; matrix products, arithmetic and copies ran while one was open for 0% of the time, Pallas kernels for 0%

commit v1 on v0

--- a/solution.py
+++ b/solution.py
@@ -126,7 +126,7 @@
     solution = jnp.zeros_like(targets)
     residual = targets
     direction = targets
-    gram = lax.psum(outer_gram(residual, residual), ("row", "col"))
+    gram = jnp.sum(lax.all_gather(outer_gram(residual, residual), ("row", "col")), axis=0)
     for iteration in range(ITERS):
         partial_value = kernel_rows(
             row_embedding,

time: 257 us -> 230 us (0.89)
  waiting for transfers between devices: 33.8 us -> 16.8 us
  blocking collectives: 182 us -> 172 us
    psum x1 -> x0, blocking collectives: 59.7 us -> none  [on_device(): gram = lax.psum(outer_gram(residual, residual), ('row', 'col'))]
    psum x1 -> x2, blocking collectives: 32.2 us -> 62.7 us  [on_device(): curvature = lax.psum(outer_gram(direction, image), ('row', 'col'))]
    all_gather x0 -> x1, blocking collectives: none -> 18.9 us  [on_device(): lax.all_gather(outer_gram(residual, residual), ('row', 'col'))]
    reduce_scatter x2, waiting for transfers between devices: 33.8 us -> 16.8 us  [on_device(): lax.psum_scatter(partial_value, 'col', scatter_dimension=1, tiled=True)]
  transfers between devices with their start and end apart: 2 -> 2, of which waited for: 2 -> 1; matrix products, arithmetic and copies ran while one was open for 0% -> 2% of each run, Pallas kernels for 0% -> 0%
where the time goes in v1:
time: 230 us; the launch traced here: 229 us
  blocking collectives  172 us (75%)
  waiting for transfers between devices  16.8 us (7%)
  between operations  15.5 us (7%)
  other arithmetic  12.1 us (5%)
  matrix products  11.6 us (5%)
    psum x2, blocking collectives, on_device(): curvature = lax.psum(outer_gram(direction, image), ('row', 'col'))  62.7 us
    psum x1, blocking collectives, on_device(): new_gram = lax.psum(outer_gram(residual, residual), ('row', 'col'))  30 us
    all_gather x2, blocking collectives, on_device(): lax.all_gather(direction, 'row', axis=1, tiled=True)  26.2 us
    all_gather x1, blocking collectives, on_device(): lax.all_gather(outer_gram(residual, residual), ('row', 'col'))  18.9 us
    reduce_scatter x2, waiting for transfers between devices, on_device(): lax.psum_scatter(partial_value, 'col', scatter_dimension=1, tiled=True)  16.8 us
    all_gather x1, blocking collectives, on_device(): lax.all_gather(embedding, 'row', axis=1, tiled=True)  12.9 us
    all_gather x1, blocking collectives, on_device(): lax.all_gather(rung_value, 'row', axis=0, tiled=True)  9.83 us
    another operation x9, other arithmetic, solve_spd(): jnp.linalg.cholesky(matrix)  6.39 us
  transfers between devices with their start and end apart: 2, of which 1 were waited for; matrix products, arithmetic and copies ran while one was open for 2% of the time, Pallas kernels for 0%

profile of v1, /device:TPU:0, one launch (start us, length us, event | category | flops | bytes accessed | tf_op | source)
XLA Modules:
  0.0 229.3 jit_solution(7015439750366681037)
XLA Ops:
  7.2 1.3 multiply_convert_fusion.1
  9.1 6.2 %all_gather.24 = bf16[64,512]{1,0:T(8,128)(2,1)S(1)} all-gather(bf16[64,128]{1,0:T(8,128)(2,1)S(1)} %fusion.4), channel_id=1, replica_groups=mesh['task'=2,'row'=4,'col'=4] {'col'}, dimensions={1}, use_global_device_ids=true | all-gather | bytes 81920 | tf_op jit(solution)/shard_map/all_gather | solution.py:117
  15.3 12.9 %all_gather.25 = bf16[64,512]{1,0:T(8,128)(2,1)S(1)} all-gather(bf16[64,128]{1,0:T(8,128)(2,1)S(1)} %fusion.4), channel_id=1, replica_groups=mesh['task'=2,'row'=4,'col'=4] {'row'}, dimensions={1}, use_global_device_ids=true | all-gather | bytes 81920 | tf_op jit(solution)/shard_map/all_gather | solution.py:121
  28.2 9.8 %all-gather.2 = bf16[4,1,128]{2,1,0:T(2,128)(2,1)S(1)} all-gather(bf16[1,1,128]{2,1,0:T(2,128)(2,1)S(1)} %convert_bitcast_fusion), channel_id=1, replica_groups=mesh['task'=2,'row'=4,'col'=4] {'row'}, dimensions={0}, use_global_device_ids=true | all-gather | bytes 1280 | tf_op jit(solution)/shard_map/all_gather | solution.py:122
  38.0 5.0 %all-gather.1 = bf16[4,1,128]{2,1,0:T(2,128)(2,1)S(1)} all-gather(bf16[1,1,128]{2,1,0:T(2,128)(2,1)S(1)} %convert_bitcast_fusion), channel_id=1, replica_groups=mesh['task'=2,'row'=4,'col'=4] {'col'}, dimensions={0}, use_global_device_ids=true | all-gather | bytes 1280 | tf_op jit(solution)/shard_map/all_gather | solution.py:118
  44.5 13.1 %all_gather.28 = f32[16,512]{1,0:T(8,128)S(1)} all-gather(f32[16,128]{1,0:T(8,128)S(1)} %copy-done.1), channel_id=1, replica_groups=mesh['task'=2,'row'=4,'col'=4] {'row'}, dimensions={1}, use_global_device_ids=true | all-gather | bytes 40960 | tf_op jit(solution)/shard_map/all_gather | solution.py:137
  59.0 1.6 convolution_bitcast_fusion
  60.8 18.9 %all-gather = f32[256,16]{1,0:T(8,128)S(1)} all-gather(f32[16,16]{1,0:T(8,128)S(1)} %fusion.37), channel_id=2, replica_groups=mesh['task'=2,'row'=4,'col'=4] {'row','col'}, dimensions={0}, use_global_device_ids=true | all-gather | bytes 17408 | tf_op jit(solution)/shard_map/all_gather | solution.py:129
  79.8 1.5 cholesky.70
  83.2 1.2 custom-call.10
  84.5 0.8 convolution_bitcast_fusion.1
  85.3 30.5 %psum.21 = f32[16,16]{0,1:T(8,128)S(1)} all-reduce(f32[16,16]{0,1:T(8,128)S(1)} %convolution_bitcast_fusion.1), channel_id=1, replica_groups=mesh['task'=2,'row'=4,'col'=4] {'row','col'}, use_global_device_ids=true, to_apply=%region_3.4 | all-reduce | flops 256 | bytes 2048 | tf_op jit(solution)/shard_map/psum | solution.py:145
  115.9 1.5 cholesky.59
  118.6 1.2 custom-call.9
  121.1 30.0 %psum.22 = f32[16,16]{1,0:T(8,128)S(1)} all-reduce(f32[16,16]{1,0:T(8,128)S(1)} %fusion.39), channel_id=1, replica_groups=mesh['task'=2,'row'=4,'col'=4] {'row','col'}, use_global_device_ids=true, to_apply=%region_7.10 | all-reduce | flops 256 | bytes 2048 | tf_op jit(solution)/shard_map/psum | solution.py:150
  151.7 13.1 %all_gather.31 = f32[16,512]{1,0:T(8,128)S(1)} all-gather(f32[16,128]{1,0:T(8,128)S(1)} %convolution_add_fusion.3), channel_id=1, replica_groups=mesh['task'=2,'row'=4,'col'=4] {'row'}, dimensions={1}, use_global_device_ids=true | all-gather | bytes 40960 | tf_op jit(solution)/shard_map/all_gather | solution.py:137
  164.8 1.6 fusion.40
  166.6 16.8 %reduce-scatter.5.cloned.1.call-done = f32[16,128]{1,0:T(8,128)} async-done(((f32[16,512]{1,0:T(8,128)}), f32[16,128]{1,0:T(8,128)}) %reduce-scatter.5.cloned.1.call-update) | async-done | bytes 8208 | tf_op jit(solution)/shard_map/reduce_scatter | solution.py:142
  183.4 0.8 fusion.28
  184.2 32.2 %psum.23 = f32[16,16]{0,1:T(8,128)S(1)} all-reduce(f32[16,16]{0,1:T(8,128)S(1)} %fusion.28), channel_id=1, replica_groups=mesh['task'=2,'row'=4,'col'=4] {'row','col'}, use_global_device_ids=true, to_apply=%region_9.12 | all-reduce | flops 256 | bytes 2048 | tf_op jit(solution)/shard_map/psum | solution.py:145
  216.5 1.5 cholesky.81
  219.3 1.2 custom-call.11
  220.8 0.8 convolution_add_fusion.2
  221.7 0.8 convolution_subtract_fusion
  (58 shorter events, 9.4 us)
Async XLA Ops:
  7.2 1.4 copy-start
  7.2 1.4 copy-start.4
  7.2 1.4 copy-start.5
  7.2 77.3 %reduce-scatter.3.cloned.1.call-start = ((), (), s32[]{:S(2)}) async-start(), calls=%async_computation.2 | async-start | bytes 40960 | tf_op jit(solution)/shard_map/reduce_scatter | solution.py:142
  15.3 12.9 %copy-start.7 = (s32[128]{0:T(128)S(1)}, s32[128]{0:T(128)}, u32[]{:S(2)}) copy-start(s32[128]{0:T(128)} %param.15) | copy-start | bytes 1540
  43.1 0.7 copy-start.6
  43.8 0.7 copy-start.1
  60.6 122.8 %reduce-scatter.5.cloned.1.call-start = ((), (), s32[]{:S(2)}) async-start(), calls=%async_computation.3 | async-start | bytes 40960 | tf_op jit(solution)/shard_map/reduce_scatter | solution.py:142
  120.1 0.7 copy-start.2
  220.8 0.8 copy-start.3
Sparse Core Ops, SparseCore 0:
  60.7 17.7 reduce-scatter.2
  166.5 16.8 reduce-scatter.4
